TPU v7x, 128 devices: a whole 4x4x4 slice. The times are simulated.
128 devices in a mesh: col: 8 (over y, z_hi), pair: 16 (over x, z_lo, core).
Axes of the slice: x: 4, y: 4, z: 4 (z_hi: 2, z_lo: 2; z = z_hi * 2 + z_lo), core: 2. Of those that a mesh axis runs over, the one named last changes fastest.
Arguments:
- integrals: bfloat16 [512, 128, 128], P('pair', 'col'), may hold values from -6 to 6
- pno_energy: float32 [512, 128], P('pair'), may hold values from 0.5 to 4
- shift: float32 [512], P('pair'), may hold values from 0.5 to 2
- intersections: bfloat16 [512, 128, 128, 128], P('pair', 'col'), may hold values from -0.09375 to 0.09375
- links: int32 [512, 128], P('pair', 'col'), may hold values from 0 to 63
- counts: int32 [512], P('pair'), may hold values from 1 to 128, as said below
- column_of: int32 [512], P('pair'), may hold values from 0 to 63
Outputs:
- amplitudes: float32 [512, 128, 128], P('pair', 'col')
- pair_energy: float32 [512], P('pair')
Inputs may be any that keep to these rules, and one draw needn't show every extreme that they name: Pair p couples through its first counts[p] slots; later slots are unused.
All inputs are finite; a program needn't handle non-finite values.
Results may differ from a plain program's by a relative error of at most 0.0012.
Values may be sent and summed in bfloat16 or wider, within the bound.
No kernel may reach another device: no remote copies, remote signals or barrier semaphores. Data moves between devices by JAX's collectives and lax.ppermute only.
A program may use at most 192 MiB of HBM per device.

v0:
```python
import jax
import jax.numpy as jnp
from jax import lax
from jax.sharding import PartitionSpec as P

COL_DEV = 8
SWEEPS = 3


def per_device(integrals, pno_energy, shift, intersections, links, counts, column_of):
    pair_dev = integrals.shape[0]
    row_count = integrals.shape[1]
    width = integrals.shape[2]
    slot_dev = intersections.shape[1]
    col_size = lax.axis_size("col")
    ncol_all = COL_DEV * col_size
    rank = lax.axis_index("col")
    row_energy = lax.dynamic_slice_in_dim(pno_energy, rank * row_count, row_count, 1)
    denom = row_energy[:, :, None] + pno_energy[:, None, :] + shift[:, None, None]
    kfloat = integrals.astype(jnp.float32)
    amplitudes = -kfloat / denom
    one_hot = (jnp.arange(ncol_all, dtype=jnp.int32)[:, None] == column_of[None, :]).astype(
        jnp.float32
    )
    own_tiles, own_links = (intersections, links)
    slot_ids = rank * slot_dev + jnp.arange(slot_dev, dtype=jnp.int32)
    own_live = (slot_ids[None, :] < counts[:, None]).astype(jnp.float32)
    for sweep in range(SWEEPS):
        contrib = jnp.dot(
            one_hot,
            amplitudes.reshape(pair_dev, row_count * width),
            precision=lax.Precision.HIGHEST,
        )
        contrib = contrib.reshape(ncol_all, row_count, width)
        totals = lax.psum(contrib, "pair")
        colamp = lax.all_gather(totals.astype(jnp.bfloat16), "col", axis=1, tiled=True)
        selected = colamp[own_links]
        left = jnp.einsum(
            "pmab,pmbc->pmac", own_tiles, selected, preferred_element_type=jnp.float32
        ).astype(jnp.bfloat16)
        right = jnp.einsum("pmac,pmdc->pmad", left, own_tiles, preferred_element_type=jnp.float32)
        partial_sum = jnp.sum(right * own_live[:, :, None, None], axis=1)
        coupled = lax.psum_scatter(partial_sum, "col", scatter_dimension=1, tiled=True)
        amplitudes = -(kfloat + coupled) / denom
    pair_energy = lax.psum(jnp.sum(kfloat * amplitudes, axis=(1, 2)), "col")
    return (amplitudes, pair_energy)


def solution(mesh):
    placed = (
        P("pair", "col", None),
        P("pair", None),
        P("pair"),
        P("pair", "col", None, None),
        P("pair", "col"),
        P("pair"),
        P("pair"),
    )
    return jax.shard_map(
        per_device,
        mesh=mesh,
        in_specs=placed,
        out_specs=(P("pair", "col", None), P("pair")),
        check_vma=False,
    )
```

profile of v0, /device:TPU:0, one launch (start us, length us, event | category | flops | bytes accessed | tf_op | source)
XLA Modules:
  0.0 745.7 jit_solution(13268401989379443307)
XLA Ops:
  7.2 0.8 constant_dynamic-slice_fusion
  8.0 1.1 fusion.18
  9.1 1.1 fusion.32
  10.3 62.5 %all-reduce.3 = bf16[64,16,128]{2,0,1:T(8,128)(2,1)} all-reduce(f32[64,16,128]{2,0,1:T(8,128)S(1)} %fusion.32), channel_id=1, replica_groups=mesh['col'=8,'pair'=16] {'pair'}, use_global_device_ids=true, to_apply=%region_0.0 | all-reduce | flops 131072 | bytes 786432 | tf_op jit(solution)/shard_map/psum | solution.py:35
  72.8 0.7 compare_select_fusion
  73.6 0.1 reshape.61
  73.7 0.7 compare_convert_fusion
  74.4 52.9 %all-gather.4.cloned.1.call-done = bf16[64,128,128]{2,0,1:T(8,128)(2,1)} async-done(((bf16[64,16,128]{2,0,1:T(8,128)(2,1)}), bf16[64,128,128]{2,0,1:T(8,128)(2,1)}) %all-gather.4.cloned.1.call-update) | async-done | bytes 2097168 | tf_op jit(solution)/shard_map/all_gather | solution.py:36
  127.3 2.9 copy.18
  130.2 13.9 %gather_fusion = bf16[512,128,128]{2,1,0:T(8,128)(2,1)} fusion(bf16[64,128,128]{2,1,0:T(8,128)(2,1)S(1)} %copy.18, s32[1024]{0:T(1024)S(1)} %pad_clamp_fusion), kind=kCustom, calls=%fused_computation | custom fusion | bytes 33556480 | tf_op jit(solution)/shard_map/gather | solution.py:37
  144.1 29.2 %multiply_reduce_fusion.2 = f32[32,128,128]{2,1,0:T(8,128)} fusion(f32[32,16]{1,0:T(8,128)S(1)} %compare_convert_fusion, bf16[32,16,128,128]{3,2,1,0:T(8,128)(2,1)} %param.10, bf16[32,16,128,128]{3,2,1,0:T(8,128)(2,1)} %bitcast.57), kind=kOutput, calls=%fused_computation.5 | convolution fusion | flops 4319608832 | bytes 35653632 | tf_op jit(solution)/shard_map/pmac,pmdc->pmad/dot_general | solution.py:41
  173.4 74.5 %reduce-scatter.4.cloned.1.call-done = f32[32,16,128]{2,1,0:T(8,128)} async-done(((f32[32,128,128]{2,1,0:T(8,128)}), f32[32,16,128]{2,1,0:T(8,128)}) %reduce-scatter.4.cloned.1.call-update) | async-done | bytes 262160 | tf_op jit(solution)/shard_map/reduce_scatter | solution.py:43
  247.9 1.1 fusion.20
  249.1 0.5 fusion.29
  249.6 59.6 %all-reduce.4 = bf16[64,16,128]{2,0,1:T(8,128)(2,1)} all-reduce(f32[64,16,128]{2,0,1:T(8,128)S(1)} %fusion.29), channel_id=1, replica_groups=mesh['col'=8,'pair'=16] {'pair'}, use_global_device_ids=true, to_apply=%region_3.0 | all-reduce | flops 131072 | bytes 786432 | tf_op jit(solution)/shard_map/psum | solution.py:35
  309.2 0.2 reduce-scatter.6.cloned.1.call-start
  309.4 51.7 %all-gather.6.cloned.1.call-done = bf16[64,128,128]{2,0,1:T(8,128)(2,1)} async-done(((bf16[64,16,128]{2,0,1:T(8,128)(2,1)}), bf16[64,128,128]{2,0,1:T(8,128)(2,1)}) %all-gather.6.cloned.1.call-update) | async-done | bytes 2097168 | tf_op jit(solution)/shard_map/all_gather | solution.py:36
  361.1 2.9 copy.22
  364.0 13.9 %gather_fusion.1 = bf16[512,128,128]{2,1,0:T(8,128)(2,1)} fusion(bf16[64,128,128]{2,1,0:T(8,128)(2,1)S(1)} %copy.22, s32[1024]{0:T(1024)S(1)} %pad_clamp_fusion), kind=kCustom, calls=%fused_computation.1 | custom fusion | bytes 33556480 | tf_op jit(solution)/shard_map/gather | solution.py:37
  377.9 29.2 %multiply_reduce_fusion.1 = f32[32,128,128]{2,1,0:T(8,128)} fusion(f32[32,16]{1,0:T(8,128)S(1)} %compare_convert_fusion, bf16[32,16,128,128]{3,2,1,0:T(8,128)(2,1)} %param.10, bf16[32,16,128,128]{3,2,1,0:T(8,128)(2,1)} %bitcast.58), kind=kOutput, calls=%fused_computation.4 | convolution fusion | flops 4319608832 | bytes 35653632 | tf_op jit(solution)/shard_map/pmac,pmdc->pmad/dot_general | solution.py:41
  407.2 74.3 %reduce-scatter.6.cloned.1.call-done = f32[32,16,128]{2,1,0:T(8,128)} async-done(((f32[32,128,128]{2,1,0:T(8,128)}), f32[32,16,128]{2,1,0:T(8,128)}) %reduce-scatter.6.cloned.1.call-update) | async-done | bytes 262160 | tf_op jit(solution)/shard_map/reduce_scatter | solution.py:43
  481.5 1.1 fusion.22
  482.7 0.5 fusion.26
  483.2 59.7 %all-reduce.5 = bf16[64,16,128]{2,0,1:T(8,128)(2,1)} all-reduce(f32[64,16,128]{2,0,1:T(8,128)S(1)} %fusion.26), channel_id=1, replica_groups=mesh['col'=8,'pair'=16] {'pair'}, use_global_device_ids=true, to_apply=%region_6.0 | all-reduce | flops 131072 | bytes 786432 | tf_op jit(solution)/shard_map/psum | solution.py:35
  542.8 0.3 reduce-scatter.8.cloned.1.call-start
  543.1 51.6 %all-gather.8.cloned.1.call-done = bf16[64,128,128]{2,0,1:T(8,128)(2,1)} async-done(((bf16[64,16,128]{2,0,1:T(8,128)(2,1)}), bf16[64,128,128]{2,0,1:T(8,128)(2,1)}) %all-gather.8.cloned.1.call-update) | async-done | bytes 2097168 | tf_op jit(solution)/shard_map/all_gather | solution.py:36
  594.8 2.9 copy.26
  597.7 13.9 %gather_fusion.2 = bf16[512,128,128]{2,1,0:T(8,128)(2,1)} fusion(bf16[64,128,128]{2,1,0:T(8,128)(2,1)S(1)} %copy.26, s32[1024]{0:T(1024)S(1)} %pad_clamp_fusion), kind=kCustom, calls=%fused_computation.2 | custom fusion | bytes 33556480 | tf_op jit(solution)/shard_map/gather | solution.py:37
  611.6 29.2 %multiply_reduce_fusion = f32[32,128,128]{2,1,0:T(8,128)} fusion(f32[32,16]{1,0:T(8,128)S(1)} %compare_convert_fusion, bf16[32,16,128,128]{3,2,1,0:T(8,128)(2,1)} %param.10, bf16[32,16,128,128]{3,2,1,0:T(8,128)(2,1)} %bitcast.56), kind=kOutput, calls=%fused_computation.3 | convolution fusion | flops 4319608832 | bytes 35653632 | tf_op jit(solution)/shard_map/pmac,pmdc->pmad/dot_general | solution.py:41
  640.8 74.3 %reduce-scatter.8.cloned.1.call-done = f32[32,16,128]{2,1,0:T(8,128)} async-done(((f32[32,128,128]{2,1,0:T(8,128)}), f32[32,16,128]{2,1,0:T(8,128)}) %reduce-scatter.8.cloned.1.call-update) | async-done | bytes 262160 | tf_op jit(solution)/shard_map/reduce_scatter | solution.py:43
  715.2 2.2 fusion.25
  717.3 21.5 %psum.31 = f32[32]{0:T(128)} all-reduce(f32[32]{0:T(128)S(1)} %get-tuple-element.2), channel_id=1, replica_groups=mesh['col'=8,'pair'=16] {'col'}, use_global_device_ids=true, to_apply=%region_10.0 | all-reduce | flops 32 | bytes 256 | tf_op jit(solution)/shard_map/psum | solution.py:45
  (21 shorter events, 0.4 us)
Async XLA Ops:
  7.2 120.1 %all-gather.4.cloned.1.call-start = ((), (), s32[]{:S(2)}) async-start(), calls=%async_computation.3 | async-start | bytes 2359296 | tf_op jit(solution)/shard_map/all_gather | solution.py:36
  72.8 175.2 %reduce-scatter.4.cloned.1.call-start = ((), (), s32[]{:S(2)}) async-start(), calls=%async_computation.4 | async-start | bytes 2359296 | tf_op jit(solution)/shard_map/reduce_scatter | solution.py:43
  144.1 103.8 %copy-start = (bf16[32,16,128]{2,1,0:T(8,128)(2,1)S(1)}, bf16[32,16,128]{2,1,0:T(8,128)(2,1)}, u32[]{:S(2)}) copy-start(bf16[32,16,128]{2,1,0:T(8,128)(2,1)} %param.7) | copy-start | bytes 393220
  144.1 103.8 %copy-start.1 = (f32[32,128]{1,0:T(8,128)S(1)}, f32[32,128]{1,0:T(8,128)}, u32[]{:S(2)}) copy-start(f32[32,128]{1,0:T(8,128)} %param.8) | copy-start | bytes 49156
  144.1 103.8 %copy-start.2 = (f32[32]{0:T(128)S(1)}, f32[32]{0:T(128)}, u32[]{:S(2)}) copy-start(f32[32]{0:T(128)} %param.9) | copy-start | bytes 388
  144.1 104.9 %copy-start.3 = (s32[32]{0:T(128)S(1)}, s32[32]{0:T(128)}, u32[]{:S(2)}) copy-start(s32[32]{0:T(128)} %param.13) | copy-start | bytes 388
  173.4 187.7 %all-gather.6.cloned.1.call-start = ((), (), s32[]{:S(2)}) async-start(), calls=%async_computation.5 | async-start | bytes 2359296 | tf_op jit(solution)/shard_map/all_gather | solution.py:36
  309.2 172.4 %reduce-scatter.6.cloned.1.call-start = ((), (), s32[]{:S(2)}) async-start(), calls=%async_computation.6 | async-start | bytes 2359296 | tf_op jit(solution)/shard_map/reduce_scatter | solution.py:43
  407.1 187.6 %all-gather.8.cloned.1.call-start = ((), (), s32[]{:S(2)}) async-start(), calls=%async_computation.7 | async-start | bytes 2359296 | tf_op jit(solution)/shard_map/all_gather | solution.py:36
  542.8 172.3 %reduce-scatter.8.cloned.1.call-start = ((), (), s32[]{:S(2)}) async-start(), calls=%async_computation.8 | async-start | bytes 2359296 | tf_op jit(solution)/shard_map/reduce_scatter | solution.py:43
Sparse Core Ops, SparseCore 0:
  72.9 54.3 all-gather.3
  173.5 74.3 reduce-scatter.3
  309.3 51.7 all-gather.5
  407.3 74.2 reduce-scatter.5
  543.0 51.7 all-gather.7
  640.9 74.1 reduce-scatter.7
where the time goes:
time: 746 us
  waiting for transfers between devices  379 us (51%)
  blocking collectives  203 us (27%)
  matrix products  89.7 us (12%)
  local copies, waits for them, and re-layouts  51.5 us (7%)
  between operations  14.2 us (2%)
    reduce_scatter x3, waiting for transfers between devices, per_device(): lax.psum_scatter(partial_sum, 'col', scatter_dimension=1, tiled=True)  223 us
    psum x3, blocking collectives, per_device(): totals = lax.psum(contrib, 'pair')  182 us
    all_gather x3, waiting for transfers between devices, per_device(): lax.all_gather(totals.astype(jnp.bfloat16), 'col', axis=1, tiled=True)  156 us
    dot_general x3, matrix products, per_device(): jnp.einsum('pmac,pmdc->pmad', left, own_tiles, preferred_element_type=jnp...  87.6 us
    gather x3, local copies, waits for them, and re-layouts, per_device(): selected = colamp[own_links]  41.7 us
    psum x1, blocking collectives, per_device(): pair_energy = lax.psum(jnp.sum(kfloat * amplitudes, axis=(1, 2)), 'col')  21.5 us
  transfers between devices with their start and end apart: 6, of which 6 were waited for; matrix products, arithmetic and copies ran while one was open for 0% of the time, Pallas kernels for 0%

commit v1 on v0

--- a/solution.py
+++ b/solution.py
@@ -33,7 +33,12 @@
         )
         contrib = contrib.reshape(ncol_all, row_count, width)
         totals = lax.psum(contrib, "pair")
-        colamp = lax.all_gather(totals.astype(jnp.bfloat16), "col", axis=1, tiled=True)
+        colamp = jnp.concatenate(
+            lax.all_to_all(
+                jnp.stack([totals.astype(jnp.bfloat16)] * lax.axis_size("col")), "col", 0, 0
+            ),
+            axis=1,
+        )
         selected = colamp[own_links]
         left = jnp.einsum(
             "pmab,pmbc->pmac", own_tiles, selected, preferred_element_type=jnp.float32

time: 746 us -> 675 us (0.905)
  waiting for transfers between devices: 379 us -> 249 us
  blocking collectives: 203 us -> 259 us
    all_gather x3 -> x0, waiting for transfers between devices: 156 us -> none  [per_device(): lax.all_gather(totals.astype(jnp.bfloat16), 'col', axis=1, tiled=True)]
    all_to_all x0 -> x2, blocking collectives: none -> 57.2 us  [per_device(): lax.all_to_all(jnp.stack([totals.astype(jnp.bfloat16)] * lax.axis_size('c...]
    all_to_all x0 -> x1, waiting for transfers between devices: none -> 23.4 us  [per_device(): lax.all_to_all(jnp.stack([totals.astype(jnp.bfloat16)] * lax.axis_size('c...]
    all_gather x3 -> x0, local copies, waits for them, and re-layouts: 8.83 us -> none  [per_device(): lax.all_gather(totals.astype(jnp.bfloat16), 'col', axis=1, tiled=True)]
  transfers between devices with their start and end apart: 6 -> 4, of which waited for: 6 -> 4; matrix products, arithmetic and copies ran while one was open for 0% -> 0% of each run, Pallas kernels for 0% -> 0%
where the time goes in v1:
time: 675 us
  blocking collectives  259 us (38%)
  waiting for transfers between devices  249 us (37%)
  matrix products  89.9 us (13%)
  local copies, waits for them, and re-layouts  48.7 us (7%)
  between operations  13.9 us (2%)
  starting transfers between devices  7.5 us (1%)
  other arithmetic  6.93 us (1%)
    reduce_scatter x3, waiting for transfers between devices, per_device(): lax.psum_scatter(partial_sum, 'col', scatter_dimension=1, tiled=True)  225 us
    psum x3, blocking collectives, per_device(): totals = lax.psum(contrib, 'pair')  180 us
    dot_general x3, matrix products, per_device(): jnp.einsum('pmac,pmdc->pmad', left, own_tiles, preferred_element_type=jnp...  87.8 us
    all_to_all x2, blocking collectives, per_device(): lax.all_to_all(jnp.stack([totals.astype(jnp.bfloat16)] * lax.axis_size('c...  57.2 us
    gather x3, local copies, waits for them, and re-layouts, per_device(): selected = colamp[own_links]  41.7 us
    all_to_all x1, waiting for transfers between devices, per_device(): lax.all_to_all(jnp.stack([totals.astype(jnp.bfloat16)] * lax.axis_size('c...  23.4 us
    psum x1, blocking collectives, per_device(): pair_energy = lax.psum(jnp.sum(kfloat * amplitudes, axis=(1, 2)), 'col')  21.5 us
  transfers between devices with their start and end apart: 4, of which 4 were waited for; matrix products, arithmetic and copies ran while one was open for 0% of the time, Pallas kernels for 0%

profile of v1, /device:TPU:0, one launch (start us, length us, event | category | flops | bytes accessed | tf_op | source)
XLA Modules:
  0.0 674.9 jit_solution(4426909340379435740)
XLA Ops:
  7.2 0.8 constant_dynamic-slice_fusion
  8.0 1.1 fusion.18
  9.1 1.1 fusion.32
  10.2 62.0 %all-reduce.3 = bf16[64,16,128]{2,0,1:T(8,128)(2,1)S(1)} all-reduce(f32[64,16,128]{2,0,1:T(8,128)S(1)} %fusion.32), channel_id=1, replica_groups=mesh['col'=8,'pair'=16] {'pair'}, use_global_device_ids=true, to_apply=%region_0.0 | all-reduce | flops 131072 | bytes 786432 | tf_op jit(solution)/shard_map/psum | solution.py:35
  72.4 1.6 stack.6
  73.9 7.4 %all-to-all-start = ((bf16[8,64,16,128]{3,2,1,0:T(8,128)(2,1)}), bf16[8,64,16,128]{3,2,1,0:T(8,128)(2,1)}, u32[]{:S(2)}, u32[]{:S(2)}) async-start(bf16[8,64,16,128]{3,2,1,0:T(8,128)(2,1)} %stack.6), calls=%async_computation | async-start | bytes 4194304 | tf_op jit(solution)/shard_map/all_to_all | solution.py:37
  81.4 0.7 compare_select_fusion
  82.2 0.7 compare_convert_fusion
  83.0 23.4 %all-to-all-done = bf16[8,64,16,128]{3,2,1,0:T(8,128)(2,1)} async-done(((bf16[8,64,16,128]{3,2,1,0:T(8,128)(2,1)}), bf16[8,64,16,128]{3,2,1,0:T(8,128)(2,1)}, u32[]{:S(2)}, u32[]{:S(2)}) %all-to-all-start) | async-done | bytes 2097184 | tf_op jit(solution)/shard_map/all_to_all | solution.py:37
  106.4 2.2 copy.21
  108.6 13.9 %gather_fusion = bf16[512,128,128]{2,1,0:T(8,128)(2,1)} fusion(bf16[64,128,128]{2,1,0:T(8,128)(2,1)S(1)} %bitcast.66, s32[1024]{0:T(1024)S(1)} %pad_clamp_fusion), kind=kCustom, calls=%fused_computation | custom fusion | bytes 33556480 | tf_op jit(solution)/shard_map/gather | solution.py:42
  122.5 29.3 %multiply_reduce_fusion.2 = f32[32,128,128]{2,1,0:T(8,128)} fusion(f32[32,16]{1,0:T(8,128)S(1)} %compare_convert_fusion, bf16[32,16,128,128]{3,2,1,0:T(8,128)(2,1)} %param.10, bf16[32,16,128,128]{3,2,1,0:T(8,128)(2,1)} %bitcast.69), kind=kOutput, calls=%fused_computation.5 | convolution fusion | flops 4319608832 | bytes 35653632 | tf_op jit(solution)/shard_map/pmac,pmdc->pmad/dot_general | solution.py:46
  151.8 77.6 %reduce-scatter.4.cloned.1.call-done = f32[32,16,128]{2,1,0:T(8,128)} async-done(((f32[32,128,128]{2,1,0:T(8,128)}), f32[32,16,128]{2,1,0:T(8,128)}) %reduce-scatter.4.cloned.1.call-update) | async-done | bytes 262160 | tf_op jit(solution)/shard_map/reduce_scatter | solution.py:48
  229.4 1.1 fusion.20
  230.6 0.5 fusion.29
  231.1 59.2 %all-reduce.4 = bf16[64,16,128]{2,0,1:T(8,128)(2,1)S(1)} all-reduce(f32[64,16,128]{2,0,1:T(8,128)S(1)} %fusion.29), channel_id=1, replica_groups=mesh['col'=8,'pair'=16] {'pair'}, use_global_device_ids=true, to_apply=%region_3.0 | all-reduce | flops 131072 | bytes 786432 | tf_op jit(solution)/shard_map/psum | solution.py:35
  290.5 0.3 stack.7
  290.8 28.6 %all_to_all.15 = bf16[8,64,16,128]{3,2,1,0:T(8,128)(2,1)S(1)} all-to-all(bf16[8,64,16,128]{3,2,1,0:T(8,128)(2,1)S(1)} %stack.7), channel_id=1, replica_groups=mesh['col'=8,'pair'=16] {'col'}, dimensions={0} | all-to-all | bytes 4194304 | tf_op jit(solution)/shard_map/all_to_all | solution.py:37
  319.4 0.6 copy.27
  320.0 13.9 %gather_fusion.1 = bf16[512,128,128]{2,1,0:T(8,128)(2,1)} fusion(bf16[64,128,128]{2,1,0:T(8,128)(2,1)S(1)} %bitcast.67, s32[1024]{0:T(1024)S(1)} %pad_clamp_fusion), kind=kCustom, calls=%fused_computation.1 | custom fusion | bytes 33556480 | tf_op jit(solution)/shard_map/gather | solution.py:42
  333.9 29.3 %multiply_reduce_fusion.1 = f32[32,128,128]{2,1,0:T(8,128)} fusion(f32[32,16]{1,0:T(8,128)S(1)} %compare_convert_fusion, bf16[32,16,128,128]{3,2,1,0:T(8,128)(2,1)} %param.10, bf16[32,16,128,128]{3,2,1,0:T(8,128)(2,1)} %bitcast.70), kind=kOutput, calls=%fused_computation.4 | convolution fusion | flops 4319608832 | bytes 35653632 | tf_op jit(solution)/shard_map/pmac,pmdc->pmad/dot_general | solution.py:46
  363.2 74.0 %reduce-scatter.6.cloned.1.call-done = f32[32,16,128]{2,1,0:T(8,128)} async-done(((f32[32,128,128]{2,1,0:T(8,128)}), f32[32,16,128]{2,1,0:T(8,128)}) %reduce-scatter.6.cloned.1.call-update) | async-done | bytes 262160 | tf_op jit(solution)/shard_map/reduce_scatter | solution.py:48
  437.2 1.1 fusion.22
  438.3 0.5 fusion.26
  438.8 59.2 %all-reduce.5 = bf16[64,16,128]{2,0,1:T(8,128)(2,1)S(1)} all-reduce(f32[64,16,128]{2,0,1:T(8,128)S(1)} %fusion.26), channel_id=1, replica_groups=mesh['col'=8,'pair'=16] {'pair'}, use_global_device_ids=true, to_apply=%region_6.0 | all-reduce | flops 131072 | bytes 786432 | tf_op jit(solution)/shard_map/psum | solution.py:35
  498.5 28.6 %all_to_all.16 = bf16[8,64,16,128]{3,2,1,0:T(8,128)(2,1)S(1)} all-to-all(bf16[8,64,16,128]{3,2,1,0:T(8,128)(2,1)S(1)} %stack.8), channel_id=1, replica_groups=mesh['col'=8,'pair'=16] {'col'}, dimensions={0} | all-to-all | bytes 4194304 | tf_op jit(solution)/shard_map/all_to_all | solution.py:37
  527.1 0.6 copy.32
  527.7 13.9 %gather_fusion.2 = bf16[512,128,128]{2,1,0:T(8,128)(2,1)} fusion(bf16[64,128,128]{2,1,0:T(8,128)(2,1)S(1)} %bitcast.65, s32[1024]{0:T(1024)S(1)} %pad_clamp_fusion), kind=kCustom, calls=%fused_computation.2 | custom fusion | bytes 33556480 | tf_op jit(solution)/shard_map/gather | solution.py:42
  541.6 29.3 %multiply_reduce_fusion = f32[32,128,128]{2,1,0:T(8,128)} fusion(f32[32,16]{1,0:T(8,128)S(1)} %compare_convert_fusion, bf16[32,16,128,128]{3,2,1,0:T(8,128)(2,1)} %param.10, bf16[32,16,128,128]{3,2,1,0:T(8,128)(2,1)} %bitcast.68), kind=kOutput, calls=%fused_computation.3 | convolution fusion | flops 4319608832 | bytes 35653632 | tf_op jit(solution)/shard_map/pmac,pmdc->pmad/dot_general | solution.py:46
  570.9 73.9 %reduce-scatter.8.cloned.1.call-done = f32[32,16,128]{2,1,0:T(8,128)} async-done(((f32[32,128,128]{2,1,0:T(8,128)}), f32[32,16,128]{2,1,0:T(8,128)}) %reduce-scatter.8.cloned.1.call-update) | async-done | bytes 262160 | tf_op jit(solution)/shard_map/reduce_scatter | solution.py:48
  644.7 2.1 fusion.25
  646.9 21.5 %psum.31 = f32[32]{0:T(128)} all-reduce(f32[32]{0:T(128)S(1)} %get-tuple-element.2), channel_id=1, replica_groups=mesh['col'=8,'pair'=16] {'col'}, use_global_device_ids=true, to_apply=%region_10.0 | all-reduce | flops 32 | bytes 256 | tf_op jit(solution)/shard_map/psum | solution.py:50
  (22 shorter events, 1.1 us)
Async XLA Ops:
  73.9 32.5 %all-to-all-start = ((bf16[8,64,16,128]{3,2,1,0:T(8,128)(2,1)}), bf16[8,64,16,128]{3,2,1,0:T(8,128)(2,1)}, u32[]{:S(2)}, u32[]{:S(2)}) async-start(bf16[8,64,16,128]{3,2,1,0:T(8,128)(2,1)} %stack.6), calls=%async_computation | async-start | bytes 4194304 | tf_op jit(solution)/shard_map/all_to_all | solution.py:37
  81.3 148.1 %reduce-scatter.4.cloned.1.call-start = ((), (), s32[]{:S(2)}) async-start(), calls=%async_computation.6 | async-start | bytes 2359296 | tf_op jit(solution)/shard_map/reduce_scatter | solution.py:48
  122.5 107.0 %copy-start = (bf16[32,16,128]{2,1,0:T(8,128)(2,1)S(1)}, bf16[32,16,128]{2,1,0:T(8,128)(2,1)}, u32[]{:S(2)}) copy-start(bf16[32,16,128]{2,1,0:T(8,128)(2,1)} %param.7) | copy-start | bytes 393220
  122.5 107.0 %copy-start.1 = (f32[32,128]{1,0:T(8,128)S(1)}, f32[32,128]{1,0:T(8,128)}, u32[]{:S(2)}) copy-start(f32[32,128]{1,0:T(8,128)} %param.8) | copy-start | bytes 49156
  122.5 107.0 %copy-start.2 = (f32[32]{0:T(128)S(1)}, f32[32]{0:T(128)}, u32[]{:S(2)}) copy-start(f32[32]{0:T(128)} %param.9) | copy-start | bytes 388
  122.5 108.1 %copy-start.3 = (s32[32]{0:T(128)S(1)}, s32[32]{0:T(128)}, u32[]{:S(2)}) copy-start(s32[32]{0:T(128)} %param.13) | copy-start | bytes 388
  151.8 285.4 %reduce-scatter.6.cloned.1.call-start = ((), (), s32[]{:S(2)}) async-start(), calls=%async_computation.7 | async-start | bytes 2359296 | tf_op jit(solution)/shard_map/reduce_scatter | solution.py:48
  363.2 281.6 %reduce-scatter.8.cloned.1.call-start = ((), (), s32[]{:S(2)}) async-start(), calls=%async_computation.8 | async-start | bytes 2359296 | tf_op jit(solution)/shard_map/reduce_scatter | solution.py:48
Sparse Core Ops, SparseCore 0:
  151.9 77.4 reduce-scatter.3
  363.3 73.8 reduce-scatter.5
  571.0 73.7 reduce-scatter.7
